TPU v7x, 256 devices: a whole 4x4x8 slice. The times are simulated.
256 devices in a mesh: section: 8 (over x, core), dp: 32 (over y, z).
Axes of the slice: x: 4, y: 4, z: 8, core: 2. Of those that a mesh axis runs over, the one named last changes fastest.
Arguments:
- resid_in: bfloat16 [4, 1024, 2048], P(None, 'dp'), may hold values from -10 to 10
- dest_row: int32 [4, 1024], replicated, may hold values from 0 to 1023, as said below
- doc_ids: int32 [4, 1024], P(None, 'dp'), may hold values from 0 to 1023, as said below
- cotangent: bfloat16 [4, 1024, 2048], P(None, 'dp'), may hold values from -0.119628906 to 0.119628906
- gain: float32 [8, 2048], P('section'), may hold values from 0.5 to 1.5
- steer: float32 [8, 2048], P('section'), may hold values from -3 to 3
- w_query: bfloat16 [8, 2048, 1024], P('section', 'dp'), may hold values from -1 to 1
- w_keyval: bfloat16 [8, 2048, 512], P('section', 'dp'), may hold values from -1 to 1
- w_out: bfloat16 [8, 1024, 2048], P('section', None, 'dp'), may hold values from -0.1875 to 0.1875
Outputs:
- hidden_out: bfloat16 [8, 4, 1024, 2048], P('section', None, 'dp')
- grad_steer: float32 [8, 2048], P('section')
Inputs may be any that keep to these rules, and one draw needn't show every extreme that they name: Each row of dest_row is a permutation of 0 to 1023. Counting the tokens of one aligned block of 32 input tokens that go to one aligned block of 32 packed rows, no count exceeds 2, and some reach it in every micro-batch. doc_ids never falls along a row; every value is a row index r at which doc_ids equals r; each aligned block of 32 rows begins a document, so no document crosses such a block.
All inputs are finite; a program needn't handle non-finite values.
Results may differ from a plain program's by a relative error of at most 0.02.
Values may be sent and summed in bfloat16 or wider, within the bound.
No kernel may reach another device: no remote copies, remote signals or barrier semaphores. Data moves between devices by JAX's collectives and lax.ppermute only.
A program may use at most 64 MiB of HBM per device.

v0:
```python
import jax
import jax.numpy as jnp
from jax import lax
from jax.sharding import PartitionSpec as P

HD = 64
ROPE_BASE = 500000.0
EPSILON = 1e-05
MASKED = -1e30


def shifted(block, axis, distance):
    devices = range(lax.axis_size(axis))
    route = [(i - distance, i) for i in devices if i - distance in devices]
    return lax.ppermute(block, axis, route)


def rotate(values, positions):
    half_size = values.shape[-1] // 2
    freq_index = jnp.arange(half_size, dtype=jnp.float32)
    inverse = ROPE_BASE ** (-2.0 * freq_index / values.shape[-1])
    angles = positions.astype(jnp.float32)[:, None] * inverse[None, :]
    cosine = jnp.cos(angles)[:, None, :]
    sine_part = jnp.sin(angles)[:, None, :]
    first_half = values[..., :half_size]
    second = values[..., half_size:]
    return jnp.concatenate(
        [first_half * cosine - second * sine_part, second * cosine + first_half * sine_part],
        axis=-1,
    )


def layer(hidden_in, steering, gain_row, w_query, w_keyval, w_out, positions, documents):
    row_count = hidden_in.shape[0]
    head_size = HD
    kv_heads = w_keyval.shape[1] // (2 * head_size)
    query_heads = w_query.shape[1] // head_size
    group_size = query_heads // kv_heads
    residual = hidden_in.astype(jnp.float32) + steering
    normed = (
        residual
        * lax.rsqrt(jnp.mean(residual * residual, axis=-1, keepdims=True) + EPSILON)
        * gain_row
    ).astype(jnp.bfloat16)
    queries = jnp.dot(normed, w_query, preferred_element_type=jnp.float32).reshape(
        row_count, query_heads, head_size
    )
    keyval = jnp.dot(normed, w_keyval, preferred_element_type=jnp.float32)
    key_rows = rotate(
        keyval[:, : kv_heads * head_size].reshape(row_count, kv_heads, head_size), positions
    ).astype(jnp.bfloat16)
    values = (
        keyval[:, kv_heads * head_size :]
        .reshape(row_count, kv_heads, head_size)
        .astype(jnp.bfloat16)
    )
    queries = (
        rotate(queries, positions)
        .astype(jnp.bfloat16)
        .reshape(row_count, kv_heads, group_size, head_size)
    )
    scores = jnp.einsum(
        "rkgd,skd->kgrs", queries, key_rows, preferred_element_type=jnp.float32
    ) * head_size ** (-0.5)
    row_index = jnp.arange(row_count)
    allowed = (documents[:, None] == documents[None, :]) & (
        row_index[:, None] >= row_index[None, :]
    )
    scores = jnp.where(allowed[None, None], scores, MASKED)
    peak = jnp.max(scores, axis=-1, keepdims=True)
    weights = jnp.exp(scores - peak)
    weights = (weights / jnp.sum(weights, axis=-1, keepdims=True)).astype(jnp.bfloat16)
    mixed_heads = jnp.einsum(
        "kgrs,skd->rkgd", weights, values, preferred_element_type=jnp.float32
    ).astype(jnp.bfloat16)
    mixed_heads = mixed_heads.reshape(row_count, query_heads * head_size)
    return (residual + jnp.dot(mixed_heads, w_out, preferred_element_type=jnp.float32)).astype(
        jnp.bfloat16
    )


def plan_slots(target, device, row_count, capacity, dp_count):
    target_grid = target.reshape(dp_count, row_count)
    target_dev = target_grid // row_count
    target_off = target_grid % row_count
    row_order = jnp.arange(row_count, dtype=jnp.int32)
    matching = target_dev[:, :, None] == target_dev[:, None, :]
    earlier = row_order[None, :] < row_order[:, None]
    rank_ids = jnp.sum((matching & earlier[None]).astype(jnp.int32), axis=2)
    slot_ids = target_dev * capacity + rank_ids
    own_slot = lax.dynamic_index_in_dim(slot_ids, device, 0, keepdims=False)
    column_ids = jnp.arange(dp_count, dtype=jnp.int32)[:, None] * capacity + rank_ids
    landing = (target_dev == device)[None] & (target_off[None] == row_order[:, None, None])
    source_col = jnp.sum(jnp.where(landing, column_ids[None], 0), axis=(1, 2))
    return (own_slot, source_col)


def pack_rows(source_rows, own_slot, slot_count):
    selector = (jnp.arange(slot_count, dtype=jnp.int32)[:, None] == own_slot[None, :]).astype(
        jnp.bfloat16
    )
    return jnp.dot(selector, source_rows, preferred_element_type=jnp.float32).astype(jnp.bfloat16)


def unpack_rows(arrived, source_col):
    selector = (
        source_col[:, None] == jnp.arange(arrived.shape[0], dtype=jnp.int32)[None, :]
    ).astype(jnp.bfloat16)
    return jnp.dot(selector, arrived, preferred_element_type=jnp.float32).astype(jnp.bfloat16)


def body(resid_in, dest_row, doc_ids, cotangent, gain, steer, w_query, w_keyval, w_out):
    dp_count = lax.axis_size("dp")
    section_count = lax.axis_size("section")
    device = lax.axis_index("dp")
    section_idx = lax.axis_index("section")
    micro_count, row_count, width = resid_in.shape
    capacity = row_count // dp_count + 1
    slot_count = dp_count * capacity
    full_query, full_keyval, full_out = (
        lax.all_gather(w_query[0], "dp", axis=0, tiled=True),
        lax.all_gather(w_keyval[0], "dp", axis=0, tiled=True),
        lax.all_gather(w_out[0], "dp", axis=1, tiled=True),
    )
    gain_row = gain[0]
    steering = steer[0]
    plans = [
        plan_slots(dest_row[micro_idx], device, row_count, capacity, dp_count)
        for micro_idx in range(micro_count)
    ]
    pieces = []
    for micro_idx in range(micro_count):
        packed = pack_rows(resid_in[micro_idx], plans[micro_idx][0], slot_count).reshape(
            dp_count, capacity, width
        )
        arrived = lax.all_to_all(packed, "dp", split_axis=0, concat_axis=0, tiled=True)
        pieces.append(unpack_rows(arrived.reshape(slot_count, width), plans[micro_idx][1]))
    grouped = jnp.stack(pieces)
    global_rows = device * row_count + jnp.arange(row_count, dtype=jnp.int32)
    position_table = global_rows[None, :] - doc_ids

    def run_layer(hidden_in, steer_vec, positions, documents):
        return layer(
            hidden_in, steer_vec, gain_row, full_query, full_keyval, full_out, positions, documents
        )

    zero_block = jnp.zeros((row_count, width), jnp.bfloat16)
    step_count = micro_count + section_count - 1

    def forward_step(carry, step_idx):
        incoming, kept, produced = carry
        micro_idx = step_idx - section_idx
        active = (micro_idx >= 0) & (micro_idx < micro_count)
        chosen = jnp.clip(micro_idx, 0, micro_count - 1)
        first_in = lax.dynamic_index_in_dim(grouped, chosen, 0, keepdims=False)
        hidden_in = jnp.where(section_idx == 0, first_in, incoming)
        positions = lax.dynamic_index_in_dim(position_table, chosen, 0, keepdims=False)
        documents = lax.dynamic_index_in_dim(doc_ids, chosen, 0, keepdims=False)
        hidden_new = lax.cond(
            active, lambda: run_layer(hidden_in, steering, positions, documents), lambda: zero_block
        )
        old_kept = lax.dynamic_index_in_dim(kept, chosen, 0, keepdims=False)
        kept = lax.dynamic_update_index_in_dim(
            kept, jnp.where(active, hidden_in, old_kept), chosen, 0
        )
        old_out = lax.dynamic_index_in_dim(produced, chosen, 0, keepdims=False)
        produced = lax.dynamic_update_index_in_dim(
            produced, jnp.where(active, hidden_new, old_out), chosen, 0
        )
        sent = shifted(hidden_new, "section", 1)
        return ((sent, kept, produced), None)

    empty_stack = jnp.zeros((micro_count, row_count, width), jnp.bfloat16)
    (unused_in, kept, produced), unused_ys = lax.scan(
        forward_step,
        (zero_block, empty_stack, empty_stack),
        jnp.arange(step_count, dtype=jnp.int32),
    )

    def backward_step(carry, step_idx):
        incoming, grad_sum = carry
        micro_idx = step_idx - (section_count - 1 - section_idx)
        active = (micro_idx >= 0) & (micro_idx < micro_count)
        chosen = jnp.clip(micro_idx, 0, micro_count - 1)
        last_in = lax.dynamic_index_in_dim(cotangent, chosen, 0, keepdims=False)
        upstream = jnp.where(section_idx == section_count - 1, last_in, incoming)
        positions = lax.dynamic_index_in_dim(position_table, chosen, 0, keepdims=False)
        documents = lax.dynamic_index_in_dim(doc_ids, chosen, 0, keepdims=False)
        saved_in = lax.dynamic_index_in_dim(kept, chosen, 0, keepdims=False)

        def differentiate():

            def local(hidden_in, steer_vec):
                return run_layer(hidden_in, steer_vec, positions, documents)

            unused_out, pullback = jax.vjp(local, saved_in, steering)
            return pullback(upstream)

        grad_in, steer_part = lax.cond(
            active, differentiate, lambda: (zero_block, jnp.zeros_like(steering))
        )
        sent = shifted(grad_in, "section", -1)
        return ((sent, grad_sum + steer_part), None)

    (unused_grad, grad_sum), unused_zs = lax.scan(
        backward_step,
        (zero_block, jnp.zeros_like(steering)),
        jnp.arange(step_count, dtype=jnp.int32),
    )
    total = lax.psum(grad_sum, "dp")
    return (produced[None], total[None])


def solution(mesh):
    in_specs = (
        P(None, "dp", None),
        P(),
        P(None, "dp"),
        P(None, "dp", None),
        P("section", None),
        P("section", None),
        P("section", "dp", None),
        P("section", "dp", None),
        P("section", None, "dp"),
    )
    out_specs = (P("section", None, "dp", None), P("section", None))
    return jax.shard_map(body, mesh=mesh, in_specs=in_specs, out_specs=out_specs, check_vma=False)
```

profile of v0, /device:TPU:0, one launch (start us, length us, event | category | flops | bytes accessed | tf_op | source)
XLA Modules:
  0.0 934.9 jit_solution(14943596170563933842)
XLA Ops:
  15.6 9.8 %all-to-all-start = ((bf16[32,2,2048]{2,1,0:T(2,128)(2,1)}), bf16[32,2,2048]{2,1,0:T(2,128)(2,1)S(1)}, u32[]{:S(2)}, u32[]{:S(2)}) async-start(bf16[32,2,2048]{2,1,0:T(2,128)(2,1)} %reshape.889), calls=%async_computation | async-start | bytes 524288 | tf_op jit(solution)/shard_map/all_to_all | solution.py:136
  29.3 9.8 %all-to-all-done = bf16[32,2,2048]{2,1,0:T(2,128)(2,1)S(1)} async-done(((bf16[32,2,2048]{2,1,0:T(2,128)(2,1)}), bf16[32,2,2048]{2,1,0:T(2,128)(2,1)S(1)}, u32[]{:S(2)}, u32[]{:S(2)}) %all-to-all-start) | async-done | bytes 262176 | tf_op jit(solution)/shard_map/all_to_all | solution.py:136
  46.1 10.0 %all-to-all-done.1 = bf16[32,2,2048]{2,1,0:T(2,128)(2,1)S(1)} async-done(((bf16[32,2,2048]{2,1,0:T(2,128)(2,1)}), bf16[32,2,2048]{2,1,0:T(2,128)(2,1)S(1)}, u32[]{:S(2)}, u32[]{:S(2)}) %all-to-all-start.1) | async-done | bytes 262176 | tf_op jit(solution)/shard_map/all_to_all | solution.py:136
  62.5 12.0 %all-to-all-done.2 = bf16[32,2,2048]{2,1,0:T(2,128)(2,1)S(1)} async-done(((bf16[32,2,2048]{2,1,0:T(2,128)(2,1)}), bf16[32,2,2048]{2,1,0:T(2,128)(2,1)S(1)}, u32[]{:S(2)}, u32[]{:S(2)}) %all-to-all-start.2) | async-done | bytes 262176 | tf_op jit(solution)/shard_map/all_to_all | solution.py:136
  82.6 10.3 %all-to-all-done.3 = bf16[32,2,2048]{2,1,0:T(2,128)(2,1)S(1)} async-done(((bf16[32,2,2048]{2,1,0:T(2,128)(2,1)}), bf16[32,2,2048]{2,1,0:T(2,128)(2,1)S(1)}, u32[]{:S(2)}, u32[]{:S(2)}) %all-to-all-start.3) | async-done | bytes 262176 | tf_op jit(solution)/shard_map/all_to_all | solution.py:136
  106.4 75.2 %all-gather.9.cloned.1.call-done = bf16[1,2048,1024]{2,1,0:T(8,128)(2,1)} async-done(((bf16[1,64,1024]{2,1,0:T(8,128)(2,1)}), bf16[1,2048,1024]{2,1,0:T(8,128)(2,1)}) %all-gather.9.cloned.1.call-update) | async-done | bytes 4194320 | tf_op jit(solution)/shard_map/all_gather | solution.py:121
  188.2 71.0 %all-gather.7.cloned.1.call-done = bf16[1,2048,512]{2,1,0:T(8,128)(2,1)} async-done(((bf16[1,64,512]{2,1,0:T(8,128)(2,1)}), bf16[1,2048,512]{2,1,0:T(8,128)(2,1)}) %all-gather.7.cloned.1.call-update) | async-done | bytes 2097168 | tf_op jit(solution)/shard_map/all_gather | solution.py:122
  259.3 156.2 %while.30 = (s32[]{:T(128)}, bf16[32,2048]{1,0:T(8,128)(2,1)S(1)}, bf16[4,32,2048]{2,1,0:T(8,128)(2,1)S(1)}, bf16[4,32,2048]{2,1,0:T(8,128)(2,1)S(1)}, s32[11]{0...) while((s32[]{:T(128)}, bf16[32,2048]{1,0:T(8,128)(2,1)S(1)}, ...), condition=%wide.region_14.15_spmd, body=%wide.region_8.14_spmd.sunk | while | flops 343888544 | bytes 14992390 | solution.py:174
  260.6 11.3 %conditional.5 = (bf16[32,2048]{1,0:T(8,128)(2,1)S(1)}) conditional(s32[]{:T(128)} %convert_element_type.419, () %tuple.130, (bf16[32,2048]{1,0:T(8,128)(2,1)S(1)}, f32[1,2048]{1,0:T(1,128)S(1)}, f32[1,2048]{1,0:T(1,128)S(1)}, bf16[2048,512]{1,0:T(8,128)(2,1)}, s32[4,32]{1,0:T(4,128)}, /*index=5*/s32[]{:T(128)}, s32[4,32]{1,0:T(4,128)}, ...), branch_computations={%region_9.9_spmd, %region_10.13_spmd} | conditional | flops 343691936 | bytes 12894860 | solution.py:159
  275.6 11.3 %conditional.5 = (bf16[32,2048]{1,0:T(8,128)(2,1)S(1)}) conditional(s32[]{:T(128)} %convert_element_type.419, () %tuple.130, (bf16[32,2048]{1,0:T(8,128)(2,1)S(1)}, f32[1,2048]{1,0:T(1,128)S(1)}, f32[1,2048]{1,0:T(1,128)S(1)}, bf16[2048,512]{1,0:T(8,128)(2,1)}, s32[4,32]{1,0:T(4,128)}, /*index=5*/s32[]{:T(128)}, s32[4,32]{1,0:T(4,128)}, ...), branch_computations={%region_9.9_spmd, %region_10.13_spmd} | conditional | flops 343691936 | bytes 12894860 | solution.py:159
  291.5 11.3 %conditional.5 = (bf16[32,2048]{1,0:T(8,128)(2,1)S(1)}) conditional(s32[]{:T(128)} %convert_element_type.419, () %tuple.130, (bf16[32,2048]{1,0:T(8,128)(2,1)S(1)}, f32[1,2048]{1,0:T(1,128)S(1)}, f32[1,2048]{1,0:T(1,128)S(1)}, bf16[2048,512]{1,0:T(8,128)(2,1)}, s32[4,32]{1,0:T(4,128)}, /*index=5*/s32[]{:T(128)}, s32[4,32]{1,0:T(4,128)}, ...), branch_computations={%region_9.9_spmd, %region_10.13_spmd} | conditional | flops 343691936 | bytes 12894860 | solution.py:159
  308.0 11.3 %conditional.5 = (bf16[32,2048]{1,0:T(8,128)(2,1)S(1)}) conditional(s32[]{:T(128)} %convert_element_type.419, () %tuple.130, (bf16[32,2048]{1,0:T(8,128)(2,1)S(1)}, f32[1,2048]{1,0:T(1,128)S(1)}, f32[1,2048]{1,0:T(1,128)S(1)}, bf16[2048,512]{1,0:T(8,128)(2,1)}, s32[4,32]{1,0:T(4,128)}, /*index=5*/s32[]{:T(128)}, s32[4,32]{1,0:T(4,128)}, ...), branch_computations={%region_9.9_spmd, %region_10.13_spmd} | conditional | flops 343691936 | bytes 12894860 | solution.py:159
  327.0 16.6 %collective-permute-start = (bf16[32,2048]{1,0:T(8,128)(2,1)S(1)}, bf16[32,2048]{1,0:T(8,128)(2,1)S(1)}, u32[]{:S(2)}, u32[]{:S(2)}) collective-permute-start(bf16[32,2048]{1,0:T(8,128)(2,1)S(1)} %get-tuple-element.1094), channel_id=1, source_target_pairs={{0,32},{32,64},{64,96},{96,128},{128,160},{160,192},{192,224},{1,3... | collective-permute-start | bytes 393224 | tf_op jit(solution)/shard_map/while/body/eval_jaxpr/ppermute | solution.py:15
  353.6 16.6 %collective-permute-start = (bf16[32,2048]{1,0:T(8,128)(2,1)S(1)}, bf16[32,2048]{1,0:T(8,128)(2,1)S(1)}, u32[]{:S(2)}, u32[]{:S(2)}) collective-permute-start(bf16[32,2048]{1,0:T(8,128)(2,1)S(1)} %get-tuple-element.1094), channel_id=1, source_target_pairs={{0,32},{32,64},{64,96},{96,128},{128,160},{160,192},{192,224},{1,3... | collective-permute-start | bytes 393224 | tf_op jit(solution)/shard_map/while/body/eval_jaxpr/ppermute | solution.py:15
  380.2 10.2 %collective-permute-start = (bf16[32,2048]{1,0:T(8,128)(2,1)S(1)}, bf16[32,2048]{1,0:T(8,128)(2,1)S(1)}, u32[]{:S(2)}, u32[]{:S(2)}) collective-permute-start(bf16[32,2048]{1,0:T(8,128)(2,1)S(1)} %get-tuple-element.1094), channel_id=1, source_target_pairs={{0,32},{32,64},{64,96},{96,128},{128,160},{160,192},{192,224},{1,3... | collective-permute-start | bytes 393224 | tf_op jit(solution)/shard_map/while/body/eval_jaxpr/ppermute | solution.py:15
  400.4 14.2 %collective-permute-start = (bf16[32,2048]{1,0:T(8,128)(2,1)S(1)}, bf16[32,2048]{1,0:T(8,128)(2,1)S(1)}, u32[]{:S(2)}, u32[]{:S(2)}) collective-permute-start(bf16[32,2048]{1,0:T(8,128)(2,1)S(1)} %get-tuple-element.1094), channel_id=1, source_target_pairs={{0,32},{32,64},{64,96},{96,128},{128,160},{160,192},{192,224},{1,3... | collective-permute-start | bytes 393224 | tf_op jit(solution)/shard_map/while/body/eval_jaxpr/ppermute | solution.py:15
  416.3 438.7 %while.31 = (s32[]{:T(128)}, bf16[32,2048]{1,0:T(8,128)(2,1)S(1)}, f32[2048]{0:T(1024)}, s32[11]{0:T(128)}, s32[]{:T(128)}, /*index=5*/pred[]{:T(512)}, bf16[4,3...) while((s32[]{:T(128)}, bf16[32,2048]{1,0:T(8,128)(2,1)S(1)}, ...), condition=%wide.region_26.27_spmd.clone, body=%wide.region_15.26_spmd.clone.sunk | while | flops 551212288 | bytes 31677904 | solution.py:205
  453.8 13.3 %collective-permute-done.1 = bf16[32,2048]{1,0:T(8,128)(2,1)S(1)} collective-permute-done((bf16[32,2048]{1,0:T(8,128)(2,1)}, bf16[32,2048]{1,0:T(8,128)(2,1)S(1)}, u32[]{:S(2)}, u32[]{:S(2)}) %collective-permute-start.1) | collective-permute-done | bytes 131104 | tf_op jit(solution)/shard_map/while/body/eval_jaxpr/ppermute | solution.py:15
  495.5 207.9 %collective-permute-done.1 = bf16[32,2048]{1,0:T(8,128)(2,1)S(1)} collective-permute-done((bf16[32,2048]{1,0:T(8,128)(2,1)}, bf16[32,2048]{1,0:T(8,128)(2,1)S(1)}, u32[]{:S(2)}, u32[]{:S(2)}) %collective-permute-start.1) | collective-permute-done | bytes 131104 | tf_op jit(solution)/shard_map/while/body/eval_jaxpr/ppermute | solution.py:15
  705.2 30.4 %conditional.6 = (bf16[32,2048]{1,0:T(8,128)(2,1)}, f32[2048]{0:T(1024)S(1)}) conditional(s32[]{:T(128)} %convert_element_type.420, () %tuple.133, (pred[]{:T(512)}, s32[]{:T(128)}, bf16[4,32,2048]{2,1,0:T(8,128)(2,1)}, bf16[32,2048]{1,0:T(8,128)(2,1)S(1)}, bf16[1024,2048]{1,0:T(8,128)(2,1)}, /*index=5*/s32[4,32]{1,0:T(4,128)}, ...), branch_computations={%region_16.16_spmd, %region_17.25_spmd} | conditional | flops 551208192 | bytes 31128680 | solution.py:199
  743.9 30.4 %conditional.6 = (bf16[32,2048]{1,0:T(8,128)(2,1)}, f32[2048]{0:T(1024)S(1)}) conditional(s32[]{:T(128)} %convert_element_type.420, () %tuple.133, (pred[]{:T(512)}, s32[]{:T(128)}, bf16[4,32,2048]{2,1,0:T(8,128)(2,1)}, bf16[32,2048]{1,0:T(8,128)(2,1)S(1)}, bf16[1024,2048]{1,0:T(8,128)(2,1)}, /*index=5*/s32[4,32]{1,0:T(4,128)}, ...), branch_computations={%region_16.16_spmd, %region_17.25_spmd} | conditional | flops 551208192 | bytes 31128680 | solution.py:199
  782.5 30.4 %conditional.6 = (bf16[32,2048]{1,0:T(8,128)(2,1)}, f32[2048]{0:T(1024)S(1)}) conditional(s32[]{:T(128)} %convert_element_type.420, () %tuple.133, (pred[]{:T(512)}, s32[]{:T(128)}, bf16[4,32,2048]{2,1,0:T(8,128)(2,1)}, bf16[32,2048]{1,0:T(8,128)(2,1)S(1)}, bf16[1024,2048]{1,0:T(8,128)(2,1)}, /*index=5*/s32[4,32]{1,0:T(4,128)}, ...), branch_computations={%region_16.16_spmd, %region_17.25_spmd} | conditional | flops 551208192 | bytes 31128680 | solution.py:199
  821.2 30.4 %conditional.6 = (bf16[32,2048]{1,0:T(8,128)(2,1)}, f32[2048]{0:T(1024)S(1)}) conditional(s32[]{:T(128)} %convert_element_type.420, () %tuple.133, (pred[]{:T(512)}, s32[]{:T(128)}, bf16[4,32,2048]{2,1,0:T(8,128)(2,1)}, bf16[32,2048]{1,0:T(8,128)(2,1)S(1)}, bf16[1024,2048]{1,0:T(8,128)(2,1)}, /*index=5*/s32[4,32]{1,0:T(4,128)}, ...), branch_computations={%region_16.16_spmd, %region_17.25_spmd} | conditional | flops 551208192 | bytes 31128680 | solution.py:199
  855.0 73.4 %psum.7 = f32[1,2048]{1,0:T(1,128)} all-reduce(f32[1,2048]{1,0:T(1,128)} %bitcast.272), channel_id=1, replica_groups=mesh['section'=8,'dp'=32] {'dp'}, use_global_device_ids=true, to_apply=%region_27.28 | all-reduce | flops 2048 | bytes 16384 | tf_op jit(solution)/shard_map/psum | solution.py:210
  (597 shorter events, 359.1 us)
Async XLA Ops:
  7.2 92.8 %all-gather.11.cloned.1.call-start = ((), (), s32[]{:S(2)}) async-start(), calls=%async_computation.6 | async-start | bytes 4325376 | tf_op jit(solution)/shard_map/all_gather | solution.py:123
  7.9 173.7 %all-gather.9.cloned.1.call-start = ((), (), s32[]{:S(2)}) async-start(), calls=%async_computation.5 | async-start | bytes 4325376 | tf_op jit(solution)/shard_map/all_gather | solution.py:121
  8.6 250.5 %all-gather.7.cloned.1.call-start = ((), (), s32[]{:S(2)}) async-start(), calls=%async_computation.4 | async-start | bytes 2162688 | tf_op jit(solution)/shard_map/all_gather | solution.py:122
  15.6 23.6 %all-to-all-start = ((bf16[32,2,2048]{2,1,0:T(2,128)(2,1)}), bf16[32,2,2048]{2,1,0:T(2,128)(2,1)S(1)}, u32[]{:S(2)}, u32[]{:S(2)}) async-start(bf16[32,2,2048]{2,1,0:T(2,128)(2,1)} %reshape.889), calls=%async_computation | async-start | bytes 524288 | tf_op jit(solution)/shard_map/all_to_all | solution.py:136
  39.2 16.9 %all-to-all-start.1 = ((bf16[32,2,2048]{2,1,0:T(2,128)(2,1)}), bf16[32,2,2048]{2,1,0:T(2,128)(2,1)S(1)}, u32[]{:S(2)}, u32[]{:S(2)}) async-start(bf16[32,2,2048]{2,1,0:T(2,128)(2,1)} %reshape.891), calls=%async_computation.1 | async-start | bytes 524288 | tf_op jit(solution)/shard_map/all_to_all | solution.py:136
  56.1 18.4 %all-to-all-start.2 = ((bf16[32,2,2048]{2,1,0:T(2,128)(2,1)}), bf16[32,2,2048]{2,1,0:T(2,128)(2,1)S(1)}, u32[]{:S(2)}, u32[]{:S(2)}) async-start(bf16[32,2,2048]{2,1,0:T(2,128)(2,1)} %reshape.893), calls=%async_computation.2 | async-start | bytes 524288 | tf_op jit(solution)/shard_map/all_to_all | solution.py:136
  74.5 18.3 %all-to-all-start.3 = ((bf16[32,2,2048]{2,1,0:T(2,128)(2,1)}), bf16[32,2,2048]{2,1,0:T(2,128)(2,1)S(1)}, u32[]{:S(2)}, u32[]{:S(2)}) async-start(bf16[32,2,2048]{2,1,0:T(2,128)(2,1)} %reshape.895), calls=%async_computation.3 | async-start | bytes 524288 | tf_op jit(solution)/shard_map/all_to_all | solution.py:136
  327.0 17.6 %collective-permute-start = (bf16[32,2048]{1,0:T(8,128)(2,1)S(1)}, bf16[32,2048]{1,0:T(8,128)(2,1)S(1)}, u32[]{:S(2)}, u32[]{:S(2)}) collective-permute-start(bf16[32,2048]{1,0:T(8,128)(2,1)S(1)} %get-tuple-element.1094), channel_id=1, source_target_pairs={{0,32},{32,64},{64,96},{96,128},{128,160},{160,192},{192,224},{1,3... | collective-permute-start | bytes 393224 | tf_op jit(solution)/shard_map/while/body/eval_jaxpr/ppermute | solution.py:15
  345.9 6.3 collective-permute-start
  353.6 17.6 %collective-permute-start = (bf16[32,2048]{1,0:T(8,128)(2,1)S(1)}, bf16[32,2048]{1,0:T(8,128)(2,1)S(1)}, u32[]{:S(2)}, u32[]{:S(2)}) collective-permute-start(bf16[32,2048]{1,0:T(8,128)(2,1)S(1)} %get-tuple-element.1094), channel_id=1, source_target_pairs={{0,32},{32,64},{64,96},{96,128},{128,160},{160,192},{192,224},{1,3... | collective-permute-start | bytes 393224 | tf_op jit(solution)/shard_map/while/body/eval_jaxpr/ppermute | solution.py:15
  372.5 6.3 collective-permute-start
  380.2 11.1 %collective-permute-start = (bf16[32,2048]{1,0:T(8,128)(2,1)S(1)}, bf16[32,2048]{1,0:T(8,128)(2,1)S(1)}, u32[]{:S(2)}, u32[]{:S(2)}) collective-permute-start(bf16[32,2048]{1,0:T(8,128)(2,1)S(1)} %get-tuple-element.1094), channel_id=1, source_target_pairs={{0,32},{32,64},{64,96},{96,128},{128,160},{160,192},{192,224},{1,3... | collective-permute-start | bytes 393224 | tf_op jit(solution)/shard_map/while/body/eval_jaxpr/ppermute | solution.py:15
  392.7 6.3 collective-permute-start
  400.4 15.1 %collective-permute-start = (bf16[32,2048]{1,0:T(8,128)(2,1)S(1)}, bf16[32,2048]{1,0:T(8,128)(2,1)S(1)}, u32[]{:S(2)}, u32[]{:S(2)}) collective-permute-start(bf16[32,2048]{1,0:T(8,128)(2,1)S(1)} %get-tuple-element.1094), channel_id=1, source_target_pairs={{0,32},{32,64},{64,96},{96,128},{128,160},{160,192},{192,224},{1,3... | collective-permute-start | bytes 393224 | tf_op jit(solution)/shard_map/while/body/eval_jaxpr/ppermute | solution.py:15
  418.8 6.3 collective-permute-start.1
  427.7 12.0 %collective-permute-start.1 = (bf16[32,2048]{1,0:T(8,128)(2,1)}, bf16[32,2048]{1,0:T(8,128)(2,1)S(1)}, u32[]{:S(2)}, u32[]{:S(2)}) collective-permute-start(bf16[32,2048]{1,0:T(8,128)(2,1)} %get-tuple-element.977), channel_id=1, source_target_pairs={{32,0},{64,32},{96,64},{128,96},{160,128},{192,160},{224,192},{33,... | collective-permute-start | bytes 393224 | tf_op jit(solution)/shard_map/while/body/eval_jaxpr/ppermute | solution.py:15
  442.2 6.5 collective-permute-start.1
  451.2 15.9 %collective-permute-start.1 = (bf16[32,2048]{1,0:T(8,128)(2,1)}, bf16[32,2048]{1,0:T(8,128)(2,1)S(1)}, u32[]{:S(2)}, u32[]{:S(2)}) collective-permute-start(bf16[32,2048]{1,0:T(8,128)(2,1)} %get-tuple-element.977), channel_id=1, source_target_pairs={{32,0},{64,32},{96,64},{128,96},{160,128},{192,160},{224,192},{33,... | collective-permute-start | bytes 393224 | tf_op jit(solution)/shard_map/while/body/eval_jaxpr/ppermute | solution.py:15
  469.6 6.5 collective-permute-start.1
  478.5 11.9 %collective-permute-start.1 = (bf16[32,2048]{1,0:T(8,128)(2,1)}, bf16[32,2048]{1,0:T(8,128)(2,1)S(1)}, u32[]{:S(2)}, u32[]{:S(2)}) collective-permute-start(bf16[32,2048]{1,0:T(8,128)(2,1)} %get-tuple-element.977), channel_id=1, source_target_pairs={{32,0},{64,32},{96,64},{128,96},{160,128},{192,160},{224,192},{33,... | collective-permute-start | bytes 393224 | tf_op jit(solution)/shard_map/while/body/eval_jaxpr/ppermute | solution.py:15
  492.9 210.5 %collective-permute-start.1 = (bf16[32,2048]{1,0:T(8,128)(2,1)}, bf16[32,2048]{1,0:T(8,128)(2,1)S(1)}, u32[]{:S(2)}, u32[]{:S(2)}) collective-permute-start(bf16[32,2048]{1,0:T(8,128)(2,1)} %get-tuple-element.977), channel_id=1, source_target_pairs={{32,0},{64,32},{96,64},{128,96},{160,128},{192,160},{224,192},{33,... | collective-permute-start | bytes 393224 | tf_op jit(solution)/shard_map/while/body/eval_jaxpr/ppermute | solution.py:15
  735.6 6.5 collective-permute-start.1
  774.2 6.5 collective-permute-start.1
  812.9 6.5 collective-permute-start.1
  (68 other events, 434.7 us)
Sparse Core Ops, SparseCore 0:
  10.6 89.3 all-gather.10
  102.5 79.0 all-gather.8
  184.2 74.8 all-gather.6
where the time goes:
time: 940 us; the launch traced here: 935 us
  waiting for transfers between devices  471 us (50%)
  starting transfers between devices  124 us (13%)
  matrix products  117 us (12%)
  blocking collectives  73.4 us (8%)
  local copies, waits for them, and re-layouts  68.4 us (7%)
  other arithmetic  50.3 us (5%)
  loops' own time  16.6 us (2%)
  between operations  14 us (1%)
    ppermute x22, waiting for transfers between devices, shifted(): return lax.ppermute(block, axis, route)  274 us
    ppermute x22, starting transfers between devices, shifted(): return lax.ppermute(block, axis, route)  99.3 us
    all_gather x1, waiting for transfers between devices, body(): lax.all_gather(w_query[0], 'dp', axis=0, tiled=True)  75.2 us
    psum x1, blocking collectives, body(): total = lax.psum(grad_sum, 'dp')  73.4 us
    all_gather x1, waiting for transfers between devices, body(): lax.all_gather(w_keyval[0], 'dp', axis=0, tiled=True)  71 us
    all_to_all x4, waiting for transfers between devices, body(): lax.all_to_all(packed, 'dp', split_axis=0, concat_axis=0, tiled=True)  42.1 us
    dot_general x12, matrix products, layer(): jnp.dot(normed, w_query, preferred_element_type=jnp.float32)  42 us
    dot_general x8, matrix products, layer(): jnp.dot(mixed_heads, w_out, preferred_element_type=jnp.float32)  26.5 us
  transfers between devices with their start and end apart: 29, of which 29 were waited for; matrix products, arithmetic and copies ran while one was open for 5% of the time, Pallas kernels for 0%

commit v1 on v0

--- a/solution.py
+++ b/solution.py
@@ -207,7 +207,10 @@
         (zero_block, jnp.zeros_like(steering)),
         jnp.arange(step_count, dtype=jnp.int32),
     )
-    total = lax.psum(grad_sum, "dp")
+    n_parts = jax.lax.psum(1, "dp")
+    total = grad_sum
+    for kk in [j0 for j0 in (1, 2, 4, 8, 16) if j0 < n_parts]:
+        total = total + jax.lax.ppermute(total, "dp", [(ii, ii ^ kk) for ii in range(n_parts)])
     return (produced[None], total[None])
 
 

time: 940 us -> 900 us (0.957)
  blocking collectives: 73.4 us -> 0 us
  waiting for transfers between devices: 471 us -> 489 us
    psum x1 -> x0, blocking collectives: 73.4 us -> none  [body(): total = lax.psum(grad_sum, 'dp')]
    ppermute x0 -> x5, waiting for transfers between devices: none -> 18.6 us  [body(): jax.lax.ppermute(total, 'dp', [(ii, ii ^ kk) for ii in range(n_parts)])]
  transfers between devices with their start and end apart: 29 -> 34, of which waited for: 29 -> 34; matrix products, arithmetic and copies ran while one was open for 5% -> 5% of each run, Pallas kernels for 0% -> 0%
where the time goes in v1:
time: 900 us; the launch traced here: 895 us
  waiting for transfers between devices  489 us (54%)
  starting transfers between devices  130 us (14%)
  matrix products  118 us (13%)
  local copies, waits for them, and re-layouts  73.2 us (8%)
  other arithmetic  54.7 us (6%)
  loops' own time  16.7 us (2%)
  between operations  14 us (2%)
    ppermute x22, waiting for transfers between devices, shifted(): return lax.ppermute(block, axis, route)  274 us
    ppermute x22, starting transfers between devices, shifted(): return lax.ppermute(block, axis, route)  99.3 us
    all_gather x1, waiting for transfers between devices, body(): lax.all_gather(w_query[0], 'dp', axis=0, tiled=True)  74.5 us
    all_gather x1, waiting for transfers between devices, body(): lax.all_gather(w_keyval[0], 'dp', axis=0, tiled=True)  71 us
    dot_general x12, matrix products, layer(): jnp.dot(normed, w_query, preferred_element_type=jnp.float32)  42.1 us
    all_to_all x4, waiting for transfers between devices, body(): lax.all_to_all(packed, 'dp', split_axis=0, concat_axis=0, tiled=True)  42 us
    dot_general x8, matrix products, layer(): jnp.dot(mixed_heads, w_out, preferred_element_type=jnp.float32)  26.5 us
    all_to_all x4, starting transfers between devices, body(): lax.all_to_all(packed, 'dp', split_axis=0, concat_axis=0, tiled=True)  24.4 us
  transfers between devices with their start and end apart: 34, of which 34 were waited for; matrix products, arithmetic and copies ran while one was open for 5% of the time, Pallas kernels for 0%

profile of v1, /device:TPU:0, one launch (start us, length us, event | category | flops | bytes accessed | tf_op | source)
XLA Modules:
  0.0 894.9 jit_solution(15918314702832459678)
XLA Ops:
  15.6 9.8 %all-to-all-start = ((bf16[32,2,2048]{2,1,0:T(2,128)(2,1)}), bf16[32,2,2048]{2,1,0:T(2,128)(2,1)S(1)}, u32[]{:S(2)}, u32[]{:S(2)}) async-start(bf16[32,2,2048]{2,1,0:T(2,128)(2,1)} %reshape.889), calls=%async_computation | async-start | bytes 524288 | tf_op jit(solution)/shard_map/all_to_all | solution.py:136
  29.3 9.8 %all-to-all-done = bf16[32,2,2048]{2,1,0:T(2,128)(2,1)S(1)} async-done(((bf16[32,2,2048]{2,1,0:T(2,128)(2,1)}), bf16[32,2,2048]{2,1,0:T(2,128)(2,1)S(1)}, u32[]{:S(2)}, u32[]{:S(2)}) %all-to-all-start) | async-done | bytes 262176 | tf_op jit(solution)/shard_map/all_to_all | solution.py:136
  46.0 10.1 %all-to-all-done.1 = bf16[32,2,2048]{2,1,0:T(2,128)(2,1)S(1)} async-done(((bf16[32,2,2048]{2,1,0:T(2,128)(2,1)}), bf16[32,2,2048]{2,1,0:T(2,128)(2,1)S(1)}, u32[]{:S(2)}, u32[]{:S(2)}) %all-to-all-start.1) | async-done | bytes 262176 | tf_op jit(solution)/shard_map/all_to_all | solution.py:136
  62.5 12.1 %all-to-all-done.2 = bf16[32,2,2048]{2,1,0:T(2,128)(2,1)S(1)} async-done(((bf16[32,2,2048]{2,1,0:T(2,128)(2,1)}), bf16[32,2,2048]{2,1,0:T(2,128)(2,1)S(1)}, u32[]{:S(2)}, u32[]{:S(2)}) %all-to-all-start.2) | async-done | bytes 262176 | tf_op jit(solution)/shard_map/all_to_all | solution.py:136
  82.5 10.0 %all-to-all-done.3 = bf16[32,2,2048]{2,1,0:T(2,128)(2,1)S(1)} async-done(((bf16[32,2,2048]{2,1,0:T(2,128)(2,1)}), bf16[32,2,2048]{2,1,0:T(2,128)(2,1)S(1)}, u32[]{:S(2)}, u32[]{:S(2)}) %all-to-all-start.3) | async-done | bytes 262176 | tf_op jit(solution)/shard_map/all_to_all | solution.py:136
  106.9 74.5 %all-gather.9.cloned.1.call-done = bf16[1,2048,1024]{2,1,0:T(8,128)(2,1)} async-done(((bf16[1,64,1024]{2,1,0:T(8,128)(2,1)}), bf16[1,2048,1024]{2,1,0:T(8,128)(2,1)}) %all-gather.9.cloned.1.call-update) | async-done | bytes 4194320 | tf_op jit(solution)/shard_map/all_gather | solution.py:121
  187.9 71.0 %all-gather.7.cloned.1.call-done = bf16[1,2048,512]{2,1,0:T(8,128)(2,1)} async-done(((bf16[1,64,512]{2,1,0:T(8,128)(2,1)}), bf16[1,2048,512]{2,1,0:T(8,128)(2,1)}) %all-gather.7.cloned.1.call-update) | async-done | bytes 2097168 | tf_op jit(solution)/shard_map/all_gather | solution.py:122
  259.1 156.2 %while.30 = (s32[]{:T(128)}, bf16[32,2048]{1,0:T(8,128)(2,1)S(1)}, bf16[4,32,2048]{2,1,0:T(8,128)(2,1)S(1)}, bf16[4,32,2048]{2,1,0:T(8,128)(2,1)S(1)}, s32[11]{0...) while((s32[]{:T(128)}, bf16[32,2048]{1,0:T(8,128)(2,1)S(1)}, ...), condition=%wide.region_14.15_spmd, body=%wide.region_8.14_spmd.sunk | while | flops 343888544 | bytes 14992390 | solution.py:174
  260.4 11.3 %conditional.5 = (bf16[32,2048]{1,0:T(8,128)(2,1)S(1)}) conditional(s32[]{:T(128)} %convert_element_type.419, () %tuple.130, (bf16[32,2048]{1,0:T(8,128)(2,1)S(1)}, f32[1,2048]{1,0:T(1,128)S(1)}, f32[1,2048]{1,0:T(1,128)S(1)}, bf16[2048,512]{1,0:T(8,128)(2,1)}, s32[4,32]{1,0:T(4,128)}, /*index=5*/s32[]{:T(128)}, s32[4,32]{1,0:T(4,128)}, ...), branch_computations={%region_9.9_spmd, %region_10.13_spmd} | conditional | flops 343691936 | bytes 12894860 | solution.py:159
  275.3 11.3 %conditional.5 = (bf16[32,2048]{1,0:T(8,128)(2,1)S(1)}) conditional(s32[]{:T(128)} %convert_element_type.419, () %tuple.130, (bf16[32,2048]{1,0:T(8,128)(2,1)S(1)}, f32[1,2048]{1,0:T(1,128)S(1)}, f32[1,2048]{1,0:T(1,128)S(1)}, bf16[2048,512]{1,0:T(8,128)(2,1)}, s32[4,32]{1,0:T(4,128)}, /*index=5*/s32[]{:T(128)}, s32[4,32]{1,0:T(4,128)}, ...), branch_computations={%region_9.9_spmd, %region_10.13_spmd} | conditional | flops 343691936 | bytes 12894860 | solution.py:159
  291.2 11.3 %conditional.5 = (bf16[32,2048]{1,0:T(8,128)(2,1)S(1)}) conditional(s32[]{:T(128)} %convert_element_type.419, () %tuple.130, (bf16[32,2048]{1,0:T(8,128)(2,1)S(1)}, f32[1,2048]{1,0:T(1,128)S(1)}, f32[1,2048]{1,0:T(1,128)S(1)}, bf16[2048,512]{1,0:T(8,128)(2,1)}, s32[4,32]{1,0:T(4,128)}, /*index=5*/s32[]{:T(128)}, s32[4,32]{1,0:T(4,128)}, ...), branch_computations={%region_9.9_spmd, %region_10.13_spmd} | conditional | flops 343691936 | bytes 12894860 | solution.py:159
  307.7 11.3 %conditional.5 = (bf16[32,2048]{1,0:T(8,128)(2,1)S(1)}) conditional(s32[]{:T(128)} %convert_element_type.419, () %tuple.130, (bf16[32,2048]{1,0:T(8,128)(2,1)S(1)}, f32[1,2048]{1,0:T(1,128)S(1)}, f32[1,2048]{1,0:T(1,128)S(1)}, bf16[2048,512]{1,0:T(8,128)(2,1)}, s32[4,32]{1,0:T(4,128)}, /*index=5*/s32[]{:T(128)}, s32[4,32]{1,0:T(4,128)}, ...), branch_computations={%region_9.9_spmd, %region_10.13_spmd} | conditional | flops 343691936 | bytes 12894860 | solution.py:159
  326.7 16.6 %collective-permute-start = (bf16[32,2048]{1,0:T(8,128)(2,1)S(1)}, bf16[32,2048]{1,0:T(8,128)(2,1)S(1)}, u32[]{:S(2)}, u32[]{:S(2)}) collective-permute-start(bf16[32,2048]{1,0:T(8,128)(2,1)S(1)} %get-tuple-element.1094), channel_id=1, source_target_pairs={{0,32},{32,64},{64,96},{96,128},{128,160},{160,192},{192,224},{1,3... | collective-permute-start | bytes 393224 | tf_op jit(solution)/shard_map/while/body/eval_jaxpr/ppermute | solution.py:15
  353.3 16.6 %collective-permute-start = (bf16[32,2048]{1,0:T(8,128)(2,1)S(1)}, bf16[32,2048]{1,0:T(8,128)(2,1)S(1)}, u32[]{:S(2)}, u32[]{:S(2)}) collective-permute-start(bf16[32,2048]{1,0:T(8,128)(2,1)S(1)} %get-tuple-element.1094), channel_id=1, source_target_pairs={{0,32},{32,64},{64,96},{96,128},{128,160},{160,192},{192,224},{1,3... | collective-permute-start | bytes 393224 | tf_op jit(solution)/shard_map/while/body/eval_jaxpr/ppermute | solution.py:15
  379.9 10.2 %collective-permute-start = (bf16[32,2048]{1,0:T(8,128)(2,1)S(1)}, bf16[32,2048]{1,0:T(8,128)(2,1)S(1)}, u32[]{:S(2)}, u32[]{:S(2)}) collective-permute-start(bf16[32,2048]{1,0:T(8,128)(2,1)S(1)} %get-tuple-element.1094), channel_id=1, source_target_pairs={{0,32},{32,64},{64,96},{96,128},{128,160},{160,192},{192,224},{1,3... | collective-permute-start | bytes 393224 | tf_op jit(solution)/shard_map/while/body/eval_jaxpr/ppermute | solution.py:15
  400.1 14.2 %collective-permute-start = (bf16[32,2048]{1,0:T(8,128)(2,1)S(1)}, bf16[32,2048]{1,0:T(8,128)(2,1)S(1)}, u32[]{:S(2)}, u32[]{:S(2)}) collective-permute-start(bf16[32,2048]{1,0:T(8,128)(2,1)S(1)} %get-tuple-element.1094), channel_id=1, source_target_pairs={{0,32},{32,64},{64,96},{96,128},{128,160},{160,192},{192,224},{1,3... | collective-permute-start | bytes 393224 | tf_op jit(solution)/shard_map/while/body/eval_jaxpr/ppermute | solution.py:15
  416.0 446.1 %while.31 = (s32[]{:T(128)}, bf16[32,2048]{1,0:T(8,128)(2,1)S(1)}, f32[2048]{0:T(1024)}, s32[11]{0:T(128)}, s32[]{:T(128)}, /*index=5*/pred[]{:T(512)}, bf16[4,3...) while((s32[]{:T(128)}, bf16[32,2048]{1,0:T(8,128)(2,1)S(1)}, ...), condition=%wide.region_26.27_spmd.clone, body=%wide.region_15.26_spmd.clone.sunk | while | flops 551212288 | bytes 31677904 | solution.py:205
  431.3 9.4 %collective-permute-done.1 = bf16[32,2048]{1,0:T(8,128)(2,1)S(1)} collective-permute-done((bf16[32,2048]{1,0:T(8,128)(2,1)}, bf16[32,2048]{1,0:T(8,128)(2,1)S(1)}, u32[]{:S(2)}, u32[]{:S(2)}) %collective-permute-start.1) | collective-permute-done | bytes 131104 | tf_op jit(solution)/shard_map/while/body/eval_jaxpr/ppermute | solution.py:15
  456.1 13.3 %collective-permute-done.1 = bf16[32,2048]{1,0:T(8,128)(2,1)S(1)} collective-permute-done((bf16[32,2048]{1,0:T(8,128)(2,1)}, bf16[32,2048]{1,0:T(8,128)(2,1)S(1)}, u32[]{:S(2)}, u32[]{:S(2)}) %collective-permute-start.1) | collective-permute-done | bytes 131104 | tf_op jit(solution)/shard_map/while/body/eval_jaxpr/ppermute | solution.py:15
  499.7 208.1 %collective-permute-done.1 = bf16[32,2048]{1,0:T(8,128)(2,1)S(1)} collective-permute-done((bf16[32,2048]{1,0:T(8,128)(2,1)}, bf16[32,2048]{1,0:T(8,128)(2,1)S(1)}, u32[]{:S(2)}, u32[]{:S(2)}) %collective-permute-start.1) | collective-permute-done | bytes 131104 | tf_op jit(solution)/shard_map/while/body/eval_jaxpr/ppermute | solution.py:15
  709.7 31.0 %conditional.6 = (bf16[32,2048]{1,0:T(8,128)(2,1)}, f32[2048]{0:T(1024)}) conditional(s32[]{:T(128)} %convert_element_type.420, () %tuple.133, (pred[]{:T(512)}, s32[]{:T(128)}, bf16[4,32,2048]{2,1,0:T(8,128)(2,1)}, bf16[32,2048]{1,0:T(8,128)(2,1)S(1)}, bf16[1024,2048]{1,0:T(8,128)(2,1)}, /*index=5*/s32[4,32]{1,0:T(4,128)}, ...), branch_computations={%region_16.16_spmd, %region_17.25_spmd} | conditional | flops 551208192 | bytes 31128680 | solution.py:199
  749.1 31.0 %conditional.6 = (bf16[32,2048]{1,0:T(8,128)(2,1)}, f32[2048]{0:T(1024)}) conditional(s32[]{:T(128)} %convert_element_type.420, () %tuple.133, (pred[]{:T(512)}, s32[]{:T(128)}, bf16[4,32,2048]{2,1,0:T(8,128)(2,1)}, bf16[32,2048]{1,0:T(8,128)(2,1)S(1)}, bf16[1024,2048]{1,0:T(8,128)(2,1)}, /*index=5*/s32[4,32]{1,0:T(4,128)}, ...), branch_computations={%region_16.16_spmd, %region_17.25_spmd} | conditional | flops 551208192 | bytes 31128680 | solution.py:199
  788.4 31.0 %conditional.6 = (bf16[32,2048]{1,0:T(8,128)(2,1)}, f32[2048]{0:T(1024)}) conditional(s32[]{:T(128)} %convert_element_type.420, () %tuple.133, (pred[]{:T(512)}, s32[]{:T(128)}, bf16[4,32,2048]{2,1,0:T(8,128)(2,1)}, bf16[32,2048]{1,0:T(8,128)(2,1)S(1)}, bf16[1024,2048]{1,0:T(8,128)(2,1)}, /*index=5*/s32[4,32]{1,0:T(4,128)}, ...), branch_computations={%region_16.16_spmd, %region_17.25_spmd} | conditional | flops 551208192 | bytes 31128680 | solution.py:199
  827.7 31.0 %conditional.6 = (bf16[32,2048]{1,0:T(8,128)(2,1)}, f32[2048]{0:T(1024)}) conditional(s32[]{:T(128)} %convert_element_type.420, () %tuple.133, (pred[]{:T(512)}, s32[]{:T(128)}, bf16[4,32,2048]{2,1,0:T(8,128)(2,1)}, bf16[32,2048]{1,0:T(8,128)(2,1)S(1)}, bf16[1024,2048]{1,0:T(8,128)(2,1)}, /*index=5*/s32[4,32]{1,0:T(4,128)}, ...), branch_computations={%region_16.16_spmd, %region_17.25_spmd} | conditional | flops 551208192 | bytes 31128680 | solution.py:199
  (611 shorter events, 387.7 us)
Async XLA Ops:
  7.2 93.2 %all-gather.11.cloned.1.call-start = ((), (), s32[]{:S(2)}) async-start(), calls=%async_computation.6 | async-start | bytes 4325376 | tf_op jit(solution)/shard_map/all_gather | solution.py:123
  7.9 173.5 %all-gather.9.cloned.1.call-start = ((), (), s32[]{:S(2)}) async-start(), calls=%async_computation.5 | async-start | bytes 4325376 | tf_op jit(solution)/shard_map/all_gather | solution.py:121
  8.6 250.3 %all-gather.7.cloned.1.call-start = ((), (), s32[]{:S(2)}) async-start(), calls=%async_computation.4 | async-start | bytes 2162688 | tf_op jit(solution)/shard_map/all_gather | solution.py:122
  15.6 23.6 %all-to-all-start = ((bf16[32,2,2048]{2,1,0:T(2,128)(2,1)}), bf16[32,2,2048]{2,1,0:T(2,128)(2,1)S(1)}, u32[]{:S(2)}, u32[]{:S(2)}) async-start(bf16[32,2,2048]{2,1,0:T(2,128)(2,1)} %reshape.889), calls=%async_computation | async-start | bytes 524288 | tf_op jit(solution)/shard_map/all_to_all | solution.py:136
  39.2 17.0 %all-to-all-start.1 = ((bf16[32,2,2048]{2,1,0:T(2,128)(2,1)}), bf16[32,2,2048]{2,1,0:T(2,128)(2,1)S(1)}, u32[]{:S(2)}, u32[]{:S(2)}) async-start(bf16[32,2,2048]{2,1,0:T(2,128)(2,1)} %reshape.891), calls=%async_computation.1 | async-start | bytes 524288 | tf_op jit(solution)/shard_map/all_to_all | solution.py:136
  56.1 18.5 %all-to-all-start.2 = ((bf16[32,2,2048]{2,1,0:T(2,128)(2,1)}), bf16[32,2,2048]{2,1,0:T(2,128)(2,1)S(1)}, u32[]{:S(2)}, u32[]{:S(2)}) async-start(bf16[32,2,2048]{2,1,0:T(2,128)(2,1)} %reshape.893), calls=%async_computation.2 | async-start | bytes 524288 | tf_op jit(solution)/shard_map/all_to_all | solution.py:136
  74.6 17.9 %all-to-all-start.3 = ((bf16[32,2,2048]{2,1,0:T(2,128)(2,1)}), bf16[32,2,2048]{2,1,0:T(2,128)(2,1)S(1)}, u32[]{:S(2)}, u32[]{:S(2)}) async-start(bf16[32,2,2048]{2,1,0:T(2,128)(2,1)} %reshape.895), calls=%async_computation.3 | async-start | bytes 524288 | tf_op jit(solution)/shard_map/all_to_all | solution.py:136
  319.1 6.3 collective-permute-start
  326.7 17.6 %collective-permute-start = (bf16[32,2048]{1,0:T(8,128)(2,1)S(1)}, bf16[32,2048]{1,0:T(8,128)(2,1)S(1)}, u32[]{:S(2)}, u32[]{:S(2)}) collective-permute-start(bf16[32,2048]{1,0:T(8,128)(2,1)S(1)} %get-tuple-element.1094), channel_id=1, source_target_pairs={{0,32},{32,64},{64,96},{96,128},{128,160},{160,192},{192,224},{1,3... | collective-permute-start | bytes 393224 | tf_op jit(solution)/shard_map/while/body/eval_jaxpr/ppermute | solution.py:15
  353.3 17.6 %collective-permute-start = (bf16[32,2048]{1,0:T(8,128)(2,1)S(1)}, bf16[32,2048]{1,0:T(8,128)(2,1)S(1)}, u32[]{:S(2)}, u32[]{:S(2)}) collective-permute-start(bf16[32,2048]{1,0:T(8,128)(2,1)S(1)} %get-tuple-element.1094), channel_id=1, source_target_pairs={{0,32},{32,64},{64,96},{96,128},{128,160},{160,192},{192,224},{1,3... | collective-permute-start | bytes 393224 | tf_op jit(solution)/shard_map/while/body/eval_jaxpr/ppermute | solution.py:15
  372.3 6.3 collective-permute-start
  379.9 11.1 %collective-permute-start = (bf16[32,2048]{1,0:T(8,128)(2,1)S(1)}, bf16[32,2048]{1,0:T(8,128)(2,1)S(1)}, u32[]{:S(2)}, u32[]{:S(2)}) collective-permute-start(bf16[32,2048]{1,0:T(8,128)(2,1)S(1)} %get-tuple-element.1094), channel_id=1, source_target_pairs={{0,32},{32,64},{64,96},{96,128},{128,160},{160,192},{192,224},{1,3... | collective-permute-start | bytes 393224 | tf_op jit(solution)/shard_map/while/body/eval_jaxpr/ppermute | solution.py:15
  400.1 15.1 %collective-permute-start = (bf16[32,2048]{1,0:T(8,128)(2,1)S(1)}, bf16[32,2048]{1,0:T(8,128)(2,1)S(1)}, u32[]{:S(2)}, u32[]{:S(2)}) collective-permute-start(bf16[32,2048]{1,0:T(8,128)(2,1)S(1)} %get-tuple-element.1094), channel_id=1, source_target_pairs={{0,32},{32,64},{64,96},{96,128},{128,160},{160,192},{192,224},{1,3... | collective-permute-start | bytes 393224 | tf_op jit(solution)/shard_map/while/body/eval_jaxpr/ppermute | solution.py:15
  419.2 6.3 collective-permute-start.1
  428.7 12.0 %collective-permute-start.1 = (bf16[32,2048]{1,0:T(8,128)(2,1)}, bf16[32,2048]{1,0:T(8,128)(2,1)S(1)}, u32[]{:S(2)}, u32[]{:S(2)}) collective-permute-start(bf16[32,2048]{1,0:T(8,128)(2,1)} %get-tuple-element.977), channel_id=1, source_target_pairs={{32,0},{64,32},{96,64},{128,96},{160,128},{192,160},{224,192},{33,... | collective-permute-start | bytes 393224 | tf_op jit(solution)/shard_map/while/body/eval_jaxpr/ppermute | solution.py:15
  443.9 6.5 collective-permute-start.1
  453.5 15.9 %collective-permute-start.1 = (bf16[32,2048]{1,0:T(8,128)(2,1)}, bf16[32,2048]{1,0:T(8,128)(2,1)S(1)}, u32[]{:S(2)}, u32[]{:S(2)}) collective-permute-start(bf16[32,2048]{1,0:T(8,128)(2,1)} %get-tuple-element.977), channel_id=1, source_target_pairs={{32,0},{64,32},{96,64},{128,96},{160,128},{192,160},{224,192},{33,... | collective-permute-start | bytes 393224 | tf_op jit(solution)/shard_map/while/body/eval_jaxpr/ppermute | solution.py:15
  472.5 6.5 collective-permute-start.1
  482.1 11.9 %collective-permute-start.1 = (bf16[32,2048]{1,0:T(8,128)(2,1)}, bf16[32,2048]{1,0:T(8,128)(2,1)S(1)}, u32[]{:S(2)}, u32[]{:S(2)}) collective-permute-start(bf16[32,2048]{1,0:T(8,128)(2,1)} %get-tuple-element.977), channel_id=1, source_target_pairs={{32,0},{64,32},{96,64},{128,96},{160,128},{192,160},{224,192},{33,... | collective-permute-start | bytes 393224 | tf_op jit(solution)/shard_map/while/body/eval_jaxpr/ppermute | solution.py:15
  497.1 210.8 %collective-permute-start.1 = (bf16[32,2048]{1,0:T(8,128)(2,1)}, bf16[32,2048]{1,0:T(8,128)(2,1)S(1)}, u32[]{:S(2)}, u32[]{:S(2)}) collective-permute-start(bf16[32,2048]{1,0:T(8,128)(2,1)} %get-tuple-element.977), channel_id=1, source_target_pairs={{32,0},{64,32},{96,64},{128,96},{160,128},{192,160},{224,192},{33,... | collective-permute-start | bytes 393224 | tf_op jit(solution)/shard_map/while/body/eval_jaxpr/ppermute | solution.py:15
  740.7 6.5 collective-permute-start.1
  780.1 6.5 collective-permute-start.1
  819.4 6.5 collective-permute-start.1
  871.4 7.6 collective-permute-start.4
  (73 other events, 458.5 us)
Sparse Core Ops, SparseCore 0:
  10.6 89.7 all-gather.10
  103.0 78.3 all-gather.8
  184.0 74.8 all-gather.6
